TPU v7x, 512 devices: a whole 4x4x16 slice. The times are simulated.
512 devices in a mesh: adapter: 64 (over y, z), mp: 8 (over x, core).
Axes of the slice: x: 4, y: 4, z: 16, core: 2. Of those that a mesh axis runs over, the one named last changes fastest.
Arguments:
- tokens: bfloat16 [24576, 8192], P('adapter', 'mp'), may hold values from -6 to 6
- cotangent: bfloat16 [24576, 1024], P('adapter', 'mp'), may hold values from -6 to 6
- value_weight: bfloat16 [8192, 1024], P('mp', 'adapter'), may hold values from -0.0625 to 0.0625
- down_store: bfloat16 [128, 8, 1024, 64], P(None, 'mp', 'adapter'), may hold values from -0.0625 to 0.0625
- down_first: float32 [128, 8, 1024, 64], P(None, 'mp', 'adapter'), may hold values from -4 to 4
- down_second: float32 [128, 8, 1024, 64], P(None, 'mp', 'adapter'), may hold values from 0.01 to 1
- up_store: bfloat16 [128, 64, 1024], P(None, 'adapter', 'mp'), may hold values from -0.75 to 0.75
- up_first: float32 [128, 64, 1024], P(None, 'adapter', 'mp'), may hold values from -4 to 4
- up_second: float32 [128, 64, 1024], P(None, 'adapter', 'mp'), may hold values from 0.01 to 1
- tile_adapter: int32 [192], replicated, may hold values from 0 to 127
- tile_length: int32 [192], replicated, may hold values from 1 to 128, as said below
- adapter_slot: int32 [128], replicated, may hold values from 0 to 127, each once
Outputs:
- projected: bfloat16 [24576, 1024], P('adapter', 'mp')
- token_gradient: bfloat16 [24576, 8192], P('adapter', 'mp')
- new_down: float32 [128, 8, 1024, 64], P(None, 'mp', 'adapter')
- new_down_first: float32 [128, 8, 1024, 64], P(None, 'mp', 'adapter')
- new_down_second: float32 [128, 8, 1024, 64], P(None, 'mp', 'adapter')
- new_up: float32 [128, 64, 1024], P(None, 'adapter', 'mp')
- new_up_first: float32 [128, 64, 1024], P(None, 'adapter', 'mp')
- new_up_second: float32 [128, 64, 1024], P(None, 'adapter', 'mp')
Inputs may be any that keep to these rules, and one draw needn't show every extreme that they name: `tile_length`: some tile is full in every draw. `adapter_slot`: each slot holds exactly one adapter.
All inputs are finite; a program needn't handle non-finite values.
Results may differ from a plain program's by a relative error of at most 0.0046.
Values may be sent and summed in bfloat16 or wider, within the bound.
No kernel may reach another device: no remote copies, remote signals or barrier semaphores. Data moves between devices by JAX's collectives and lax.ppermute only.
A program may use at most 64 MiB of HBM per device.

v0:
```python
import jax
import jax.numpy as jnp
from jax import lax
from jax.sharding import Mesh, PartitionSpec as P

TILE = 128
STEP = 100
adapter_scale = 2.0
learn_rate = 0.001
beta_one = 0.9
beta_two = 0.999
adam_eps = 1e-08


def adam_step(store, first, second, gradient):
    new_first = beta_one * first + (1.0 - beta_one) * gradient
    new_second = beta_two * second + (1.0 - beta_two) * gradient * gradient
    corr_one = 1.0 - beta_one**STEP
    corr_two = 1.0 - beta_two**STEP
    moved = store.astype(jnp.float32) - learn_rate * (new_first / corr_one) / (
        jnp.sqrt(new_second / corr_two) + adam_eps
    )
    return (moved, new_first, new_second)


ADAPTER = ("ay", "az")


def gather_along(piece, axis):
    count = lax.axis_size(axis)
    got = [piece]
    for shift in range(1, count):
        pairs = [(j, (j - shift) % count) for j in range(count)]
        got.append(lax.ppermute(piece, axis, pairs))
    ordered = jnp.roll(jnp.stack(got), lax.axis_index(axis), axis=0)
    return jnp.moveaxis(ordered, 0, 1).reshape(piece.shape[0], count * piece.shape[1])


def gather_weight(value_weight):
    return gather_along(gather_along(value_weight, "az"), "ay")


def split_adapter(mesh):
    devices = mesh.devices
    n_adapter = devices.shape[0]
    try:
        n_y = len({d.coords[1] for d in devices[:, 0]})
    except (AttributeError, IndexError, TypeError):
        n_y = 1
    if n_y < 1 or n_adapter % n_y:
        n_y = 1
    return Mesh(devices.reshape(n_y, n_adapter // n_y, devices.shape[1]), ("ay", "az", "mp"))


def shards(
    tokens,
    cotangent,
    value_weight,
    down_store,
    down_first,
    down_second,
    up_store,
    up_first,
    up_second,
    tile_adapter,
    tile_length,
    adapter_slot,
):
    tile_total = tile_adapter.shape[0]
    tok_count, feat_part = tokens.shape
    head_cols = cotangent.shape[1]
    tiles_here = tok_count // TILE
    adapter_count = adapter_slot.shape[0]
    my_index = lax.axis_index(ADAPTER)
    adapter_ids = jnp.arange(adapter_count, dtype=jnp.int32)
    tile_adapter_slot = jnp.sum(
        jnp.where(tile_adapter[:, None] == adapter_ids[None, :], adapter_slot[None, :], 0), axis=1
    )
    my_lengths = lax.dynamic_slice_in_dim(tile_length, my_index * tiles_here, tiles_here)
    active_rows = (jnp.arange(TILE)[None, :] < my_lengths[:, None]).reshape(tok_count, 1)
    masked_own = cotangent * active_rows.astype(jnp.bfloat16)
    masked_full = lax.all_gather(masked_own, "mp", axis=1, tiled=True)
    n_adapter = tile_total // tiles_here
    row_part = down_store.shape[2]
    rank = down_store.shape[3]
    sent_down = down_store[:, 0][tile_adapter_slot].reshape(tile_total, row_part * rank)
    sent_up = up_store[tile_adapter_slot].reshape(tile_total, head_cols)
    sent = jnp.concatenate([sent_down, sent_up], axis=1)
    arrived = lax.all_to_all(sent, ADAPTER, split_axis=0, concat_axis=0, tiled=True)
    arrived = arrived.reshape(n_adapter, tiles_here, row_part * rank + head_cols)
    down_panel = (
        arrived[:, :, : row_part * rank]
        .reshape(n_adapter, tiles_here, row_part, rank)
        .transpose(1, 0, 2, 3)
        .reshape(tiles_here, n_adapter * row_part, rank)
    )
    up_panel = arrived[:, :, row_part * rank :].transpose(1, 0, 2)
    w_full = gather_weight(value_weight)
    token_tiles = tokens.reshape(tiles_here, TILE, feat_part)
    frozen_part = jnp.dot(tokens, w_full, preferred_element_type=jnp.float32)
    frozen_local = lax.psum_scatter(frozen_part, "mp", scatter_dimension=1, tiled=True)
    down_part = jnp.einsum(
        "ntd,ndr->ntr", token_tiles, down_panel, preferred_element_type=jnp.float32
    )
    down_sum = lax.psum(down_part, "mp")
    down_portion = down_sum.astype(jnp.bfloat16)
    adapter_term = jnp.einsum(
        "ntr,nrv->ntv", down_portion, up_panel, preferred_element_type=jnp.float32
    ).reshape(tok_count, head_cols)
    projected = (
        (frozen_local + adapter_scale * adapter_term) * active_rows.astype(jnp.float32)
    ).astype(jnp.bfloat16)
    tile_mask = masked_own.reshape(tiles_here, TILE, head_cols)
    backward_piece = adapter_scale * jnp.einsum(
        "ntv,nrv->ntr", tile_mask, up_panel, preferred_element_type=jnp.float32
    )
    backward_portion = lax.psum(backward_piece, "mp").astype(jnp.bfloat16)
    frozen_backward = lax.dot_general(
        masked_full, w_full, (((1,), (1,)), ((), ())), preferred_element_type=jnp.float32
    )
    adapter_backward = jnp.einsum(
        "ntr,ndr->ntd", backward_portion, down_panel, preferred_element_type=jnp.float32
    ).reshape(tok_count, feat_part)
    token_gradient = (frozen_backward + adapter_backward).astype(jnp.bfloat16)
    home_down = jnp.einsum(
        "ntd,ntr->ndr", token_tiles, backward_portion, preferred_element_type=jnp.float32
    )
    local_up_weight = adapter_scale * jnp.einsum(
        "ntr,ntv->nrv", down_portion, tile_mask, preferred_element_type=jnp.float32
    )
    grads = jnp.concatenate(
        [home_down.reshape(tiles_here, n_adapter, row_part * rank), local_up_weight], axis=2
    )
    grads = lax.all_to_all(grads, ADAPTER, split_axis=1, concat_axis=0, tiled=True)
    arrived_down = grads[:, 0, : row_part * rank]
    arrived_up = grads[:, 0, row_part * rank :]
    selector = (adapter_ids[:, None] == tile_adapter_slot[None, :]).astype(jnp.float32)
    down_gradient = jnp.dot(
        selector, arrived_down.reshape(tile_total, -1), precision=lax.Precision.HIGHEST
    ).reshape(down_store.shape)
    up_gradient = jnp.dot(
        selector, arrived_up.reshape(tile_total, -1), precision=lax.Precision.HIGHEST
    ).reshape(up_store.shape)
    new_down, new_down_first, new_down_second = adam_step(
        down_store, down_first, down_second, down_gradient
    )
    new_up, new_up_first, new_up_second = adam_step(up_store, up_first, up_second, up_gradient)
    return (
        projected,
        token_gradient,
        new_down,
        new_down_first,
        new_down_second,
        new_up,
        new_up_first,
        new_up_second,
    )


def solution(mesh):
    mesh = split_adapter(mesh)
    placed = (
        P(ADAPTER, "mp"),
        P(ADAPTER, "mp"),
        P("mp", ADAPTER),
        P(None, "mp", ADAPTER, None),
        P(None, "mp", ADAPTER, None),
        P(None, "mp", ADAPTER, None),
        P(None, ADAPTER, "mp"),
        P(None, ADAPTER, "mp"),
        P(None, ADAPTER, "mp"),
        P(),
        P(),
        P(),
    )
    return jax.shard_map(
        shards,
        mesh=mesh,
        in_specs=placed,
        out_specs=(
            P(ADAPTER, "mp"),
            P(ADAPTER, "mp"),
            P(None, "mp", ADAPTER, None),
            P(None, "mp", ADAPTER, None),
            P(None, "mp", ADAPTER, None),
            P(None, ADAPTER, "mp"),
            P(None, ADAPTER, "mp"),
            P(None, ADAPTER, "mp"),
        ),
        check_vma=False,
    )
```

profile of v0, /device:TPU:6, one launch (start us, length us, event | category | flops | bytes accessed | tf_op | source)
XLA Modules:
  0.0 261.7 jit_solution(3475305058610863027)
XLA Ops:
  7.2 11.5 %collective-permute-start = (bf16[1024,16]{0,1:T(8,128)(2,1)}, bf16[1024,16]{0,1:T(8,128)(2,1)S(1)}, u32[]{:S(2)}, u32[]{:S(2)}) collective-permute-start(bf16[1024,16]{0,1:T(8,128)(2,1)} %param.14), channel_id=1, source_target_pairs={{0,120},{8,0},{16,8},{24,16},{32,24},{40,32},{48,40},{56,48},{64,5... | collective-permute-start | bytes 98312 | tf_op jit(solution)/shard_map/ppermute | solution.py:34
  18.7 3.4 %collective-permute-start.1 = (bf16[1024,16]{0,1:T(8,128)(2,1)}, bf16[1024,16]{0,1:T(8,128)(2,1)S(1)}, u32[]{:S(2)}, u32[]{:S(2)}) collective-permute-start(bf16[1024,16]{0,1:T(8,128)(2,1)} %param.14), channel_id=1, source_target_pairs={{0,112},{8,120},{16,0},{24,8},{32,16},{40,24},{48,32},{56,40},{64,... | collective-permute-start | bytes 98312 | tf_op jit(solution)/shard_map/ppermute | solution.py:34
  22.1 5.0 %collective-permute-start.2 = (bf16[1024,16]{0,1:T(8,128)(2,1)}, bf16[1024,16]{0,1:T(8,128)(2,1)S(1)}, u32[]{:S(2)}, u32[]{:S(2)}) collective-permute-start(bf16[1024,16]{0,1:T(8,128)(2,1)} %param.14), channel_id=1, source_target_pairs={{0,104},{8,112},{16,120},{24,0},{32,8},{40,16},{48,24},{56,32},{64... | collective-permute-start | bytes 98312 | tf_op jit(solution)/shard_map/ppermute | solution.py:34
  27.1 2.8 %collective-permute-start.3 = (bf16[1024,16]{0,1:T(8,128)(2,1)}, bf16[1024,16]{0,1:T(8,128)(2,1)S(1)}, u32[]{:S(2)}, u32[]{:S(2)}) collective-permute-start(bf16[1024,16]{0,1:T(8,128)(2,1)} %param.14), channel_id=1, source_target_pairs={{0,96},{8,104},{16,112},{24,120},{32,0},{40,8},{48,16},{56,24},{64... | collective-permute-start | bytes 98312 | tf_op jit(solution)/shard_map/ppermute | solution.py:34
  30.0 1.9 collective-permute-start.4
  38.1 15.8 %all-to-all-start = ((bf16[64,3,1152]{2,1,0:T(4,128)(2,1)}), bf16[64,3,1152]{2,1,0:T(4,128)(2,1)S(1)}, u32[]{:S(2)}, u32[]{:S(2)}) async-start(bf16[64,3,1152]{2,1,0:T(4,128)(2,1)} %pad_maximum_fusion.1), calls=%async_computation.1 | async-start | bytes 1179648 | tf_op jit(solution)/shard_map/all_to_all | solution.py:89
  54.0 10.4 %collective-permute-start.5 = (bf16[1024,16]{0,1:T(8,128)(2,1)S(1)}, bf16[1024,16]{0,1:T(8,128)(2,1)S(1)}, u32[]{:S(2)}, u32[]{:S(2)}) collective-permute-start(bf16[1024,16]{0,1:T(8,128)(2,1)S(1)} %copy-done.3), channel_id=1, source_target_pairs={{0,80},{8,88},{16,96},{24,104},{32,112},{40,120},{48,0},{56,8},{64... | collective-permute-start | bytes 98312 | tf_op jit(solution)/shard_map/ppermute | solution.py:34
  64.4 4.3 %collective-permute-start.6 = (bf16[1024,16]{0,1:T(8,128)(2,1)S(1)}, bf16[1024,16]{0,1:T(8,128)(2,1)S(1)}, u32[]{:S(2)}, u32[]{:S(2)}) collective-permute-start(bf16[1024,16]{0,1:T(8,128)(2,1)S(1)} %copy-done.3), channel_id=1, source_target_pairs={{0,72},{8,80},{16,88},{24,96},{32,104},{40,112},{48,120},{56,0},{6... | collective-permute-start | bytes 98312 | tf_op jit(solution)/shard_map/ppermute | solution.py:34
  68.7 9.4 %collective-permute-start.7 = (bf16[1024,16]{0,1:T(8,128)(2,1)S(1)}, bf16[1024,16]{0,1:T(8,128)(2,1)S(1)}, u32[]{:S(2)}, u32[]{:S(2)}) collective-permute-start(bf16[1024,16]{0,1:T(8,128)(2,1)S(1)} %copy-done.3), channel_id=1, source_target_pairs={{0,64},{8,72},{16,80},{24,88},{32,96},{40,104},{48,112},{56,120},{... | collective-permute-start | bytes 98312 | tf_op jit(solution)/shard_map/ppermute | solution.py:34
  78.1 3.1 %collective-permute-start.8 = (bf16[1024,16]{0,1:T(8,128)(2,1)S(1)}, bf16[1024,16]{0,1:T(8,128)(2,1)S(1)}, u32[]{:S(2)}, u32[]{:S(2)}) collective-permute-start(bf16[1024,16]{0,1:T(8,128)(2,1)S(1)} %copy-done.3), channel_id=1, source_target_pairs={{0,56},{8,64},{16,72},{24,80},{32,88},{40,96},{48,104},{56,112},{6... | collective-permute-start | bytes 98312 | tf_op jit(solution)/shard_map/ppermute | solution.py:34
  81.2 10.3 %collective-permute-start.9 = (bf16[1024,16]{0,1:T(8,128)(2,1)S(1)}, bf16[1024,16]{0,1:T(8,128)(2,1)S(1)}, u32[]{:S(2)}, u32[]{:S(2)}) collective-permute-start(bf16[1024,16]{0,1:T(8,128)(2,1)S(1)} %copy-done.3), channel_id=1, source_target_pairs={{0,48},{8,56},{16,64},{24,72},{32,80},{40,88},{48,96},{56,104},{64... | collective-permute-start | bytes 98312 | tf_op jit(solution)/shard_map/ppermute | solution.py:34
  91.5 6.7 %collective-permute-start.10 = (bf16[1024,16]{0,1:T(8,128)(2,1)S(1)}, bf16[1024,16]{0,1:T(8,128)(2,1)S(1)}, u32[]{:S(2)}, u32[]{:S(2)}) collective-permute-start(bf16[1024,16]{0,1:T(8,128)(2,1)S(1)} %copy-done.3), channel_id=1, source_target_pairs={{0,40},{8,48},{16,56},{24,64},{32,72},{40,80},{48,88},{56,96},{64,... | collective-permute-start | bytes 98312 | tf_op jit(solution)/shard_map/ppermute | solution.py:34
  98.2 1.9 collective-permute-start.11
  100.2 5.2 %collective-permute-start.12 = (bf16[1024,16]{0,1:T(8,128)(2,1)S(1)}, bf16[1024,16]{0,1:T(8,128)(2,1)S(1)}, u32[]{:S(2)}, u32[]{:S(2)}) collective-permute-start(bf16[1024,16]{0,1:T(8,128)(2,1)S(1)} %copy-done.3), channel_id=1, source_target_pairs={{0,24},{8,32},{16,40},{24,48},{32,56},{40,64},{48,72},{56,80},{64,... | collective-permute-start | bytes 98312 | tf_op jit(solution)/shard_map/ppermute | solution.py:34
  105.5 2.7 %collective-permute-start.13 = (bf16[1024,16]{0,1:T(8,128)(2,1)S(1)}, bf16[1024,16]{0,1:T(8,128)(2,1)S(1)}, u32[]{:S(2)}, u32[]{:S(2)}) collective-permute-start(bf16[1024,16]{0,1:T(8,128)(2,1)S(1)} %copy-done.3), channel_id=1, source_target_pairs={{0,16},{8,24},{16,32},{24,40},{32,48},{40,56},{48,64},{56,72},{64,... | collective-permute-start | bytes 98312 | tf_op jit(solution)/shard_map/ppermute | solution.py:34
  108.1 4.8 %collective-permute-start.14 = (bf16[1024,16]{0,1:T(8,128)(2,1)S(1)}, bf16[1024,16]{0,1:T(8,128)(2,1)S(1)}, u32[]{:S(2)}, u32[]{:S(2)}) collective-permute-start(bf16[1024,16]{0,1:T(8,128)(2,1)S(1)} %copy-done.3), channel_id=1, source_target_pairs={{0,8},{8,16},{16,24},{24,32},{32,40},{40,48},{48,56},{56,64},{64,7... | collective-permute-start | bytes 98312 | tf_op jit(solution)/shard_map/ppermute | solution.py:34
  113.4 1.8 collective-permute-done.14
  115.4 4.8 %collective-permute-start.15 = (bf16[1024,256]{0,1:T(8,128)(2,1)S(1)}, bf16[1024,256]{0,1:T(8,128)(2,1)S(1)}, u32[]{:S(2)}, u32[]{:S(2)}) collective-permute-start(bf16[1024,256]{0,1:T(8,128)(2,1)S(1)} %bitcast.143), channel_id=1, source_target_pairs={{0,384},{128,0},{256,128},{384,256},{1,385},{129,1},{257,129},{385... | collective-permute-start | bytes 1572872 | tf_op jit(solution)/shard_map/ppermute | solution.py:34
  120.3 2.5 collective-permute-start.16
  123.0 2.9 %collective-permute-start.17 = (bf16[1024,256]{0,1:T(8,128)(2,1)S(1)}, bf16[1024,256]{0,1:T(8,128)(2,1)S(1)}, u32[]{:S(2)}, u32[]{:S(2)}) collective-permute-start(bf16[1024,256]{0,1:T(8,128)(2,1)S(1)} %bitcast.145), channel_id=1, source_target_pairs={{0,128},{128,256},{256,384},{384,0},{1,129},{129,257},{257,385},{3... | collective-permute-start | bytes 1572872 | tf_op jit(solution)/shard_map/ppermute | solution.py:34
  125.9 11.5 %collective-permute-done.15 = bf16[1024,256]{0,1:T(8,128)(2,1)S(1)} collective-permute-done((bf16[1024,256]{0,1:T(8,128)(2,1)S(1)}, bf16[1024,256]{0,1:T(8,128)(2,1)S(1)}, u32[]{:S(2)}, u32[]{:S(2)}) %collective-permute-start.15) | collective-permute-done | bytes 524320 | tf_op jit(solution)/shard_map/ppermute | solution.py:34
  137.6 5.5 %collective-permute-done.17 = bf16[1024,256]{0,1:T(8,128)(2,1)S(1)} collective-permute-done((bf16[1024,256]{0,1:T(8,128)(2,1)S(1)}, bf16[1024,256]{0,1:T(8,128)(2,1)S(1)}, u32[]{:S(2)}, u32[]{:S(2)}) %collective-permute-start.17) | collective-permute-done | bytes 524320 | tf_op jit(solution)/shard_map/ppermute | solution.py:34
  146.4 22.7 %all-reduce.2 = (bf16[3,128,64]{1,2,0:T(8,128)(2,1)S(1)}, bf16[3,128,64]{1,2,0:T(8,128)(2,1)S(1)}) all-reduce(f32[3,128,64]{1,2,0:T(8,128)S(1)} %convolution_bitcast_fusion.2, f32[3,128,64]{1,2,0:T(8,128)S(1)} %convolution_multiply_fusion.2), channel_id=1, replica_groups=mesh['ay'=4,'az'=16,'mp'=8] {'mp'}, use_global_device_ids=true, to_apply=%region_2.3 | all-reduce | flops 49152 | bytes 294912 | tf_op jit(solution)/shard_map/psum | solution.py:105
  176.1 10.2 %all-to-all-start.1 = ((f32[3,64,1152]{2,0,1:T(4,128)}), f32[3,64,1152]{2,0,1:T(4,128)S(1)}, u32[]{:S(2)}, u32[]{:S(2)}) async-start(f32[3,64,1152]{2,0,1:T(4,128)} %copy.83), calls=%async_computation.2 | async-start | bytes 2359296 | tf_op jit(solution)/shard_map/all_to_all | solution.py:134
  186.4 4.0 %convolution_bitcast_fusion = f32[384,1024]{0,1:T(8,128)} fusion(bf16[1024,1024]{0,1:T(8,128)(2,1)} %bitcast.150, bf16[384,1024]{1,0:T(8,128)(2,1)S(1)} %copy-done), kind=kOutput, calls=%fused_computation.4 | convolution fusion | flops 805306368 | bytes 4456448 | tf_op jit(solution)/shard_map/dot_general | solution.py:100
  190.4 15.3 %all_gather.3 = bf16[384,1024]{1,0:T(8,128)(2,1)} all-gather(bf16[384,128]{1,0:T(8,128)(2,1)S(1)} %broadcast_multiply_fusion), channel_id=1, replica_groups=mesh['ay'=4,'az'=16,'mp'=8] {'mp'}, dimensions={1}, use_global_device_ids=true | all-gather | bytes 884736 | tf_op jit(solution)/shard_map/all_gather | solution.py:82
  206.5 3.7 %fusion = bf16[384,1024]{1,0:T(8,128)(2,1)} fusion(f32[3,128,1024]{2,1,0:T(8,128)S(1)} %fusion.19, bf16[384,1024]{1,0:T(8,128)(2,1)} %all_gather.3, bf16[1024,1024]{0,1:T(8,128)(2,1)} %bitcast.151), kind=kOutput, calls=%fused_computation.3 | convolution fusion | flops 806092800 | bytes 5242880 | tf_op jit(solution)/shard_map/dot_general | solution.py:118
  210.2 19.9 %reduce-scatter.2.cloned.1.call-done = f32[384,128]{0,1:T(8,128)} async-done(((f32[384,1024]{0,1:T(8,128)}), f32[384,128]{0,1:T(8,128)}) %reduce-scatter.2.cloned.1.call-update) | async-done | bytes 196624 | tf_op jit(solution)/shard_map/reduce_scatter | solution.py:101
  231.8 14.7 %all-to-all-done.1 = f32[3,64,1152]{2,0,1:T(4,128)S(1)} async-done(((f32[3,64,1152]{2,0,1:T(4,128)}), f32[3,64,1152]{2,0,1:T(4,128)S(1)}, u32[]{:S(2)}, u32[]{:S(2)}) %all-to-all-start.1) | async-done | bytes 884768 | tf_op jit(solution)/shard_map/all_to_all | solution.py:134
  246.5 2.1 all_to_all.21
  248.6 1.7 slice.22
  251.3 2.6 divide_subtract_fusion
  (109 shorter events, 21.9 us)
Async XLA Ops:
  7.2 138.8 %copy-start = (bf16[384,1024]{1,0:T(8,128)(2,1)S(1)}, bf16[384,1024]{1,0:T(8,128)(2,1)}, u32[]{:S(2)}) copy-start(bf16[384,1024]{1,0:T(8,128)(2,1)} %param.12) | copy-start | bytes 2359300
  7.2 46.7 %copy-start.3 = (bf16[1024,16]{0,1:T(8,128)(2,1)S(1)}, bf16[1024,16]{0,1:T(8,128)(2,1)}, u32[]{:S(2)}) copy-start(bf16[1024,16]{0,1:T(8,128)(2,1)} %param.14) | copy-start | bytes 98308
  7.2 46.7 %copy-start.7 = (s32[192]{0:T(256)S(1)}, s32[192]{0:T(256)}, u32[]{:S(2)}) copy-start(s32[192]{0:T(256)} %param.22) | copy-start | bytes 2308
  7.2 46.8 %collective-permute-start = (bf16[1024,16]{0,1:T(8,128)(2,1)}, bf16[1024,16]{0,1:T(8,128)(2,1)S(1)}, u32[]{:S(2)}, u32[]{:S(2)}) collective-permute-start(bf16[1024,16]{0,1:T(8,128)(2,1)} %param.14), channel_id=1, source_target_pairs={{0,120},{8,0},{16,8},{24,16},{32,24},{40,32},{48,40},{56,48},{64,5... | collective-permute-start | bytes 98312 | tf_op jit(solution)/shard_map/ppermute | solution.py:34
  18.7 45.6 %collective-permute-start.1 = (bf16[1024,16]{0,1:T(8,128)(2,1)}, bf16[1024,16]{0,1:T(8,128)(2,1)S(1)}, u32[]{:S(2)}, u32[]{:S(2)}) collective-permute-start(bf16[1024,16]{0,1:T(8,128)(2,1)} %param.14), channel_id=1, source_target_pairs={{0,112},{8,120},{16,0},{24,8},{32,16},{40,24},{48,32},{56,40},{64,... | collective-permute-start | bytes 98312 | tf_op jit(solution)/shard_map/ppermute | solution.py:34
  22.1 46.6 %collective-permute-start.2 = (bf16[1024,16]{0,1:T(8,128)(2,1)}, bf16[1024,16]{0,1:T(8,128)(2,1)S(1)}, u32[]{:S(2)}, u32[]{:S(2)}) collective-permute-start(bf16[1024,16]{0,1:T(8,128)(2,1)} %param.14), channel_id=1, source_target_pairs={{0,104},{8,112},{16,120},{24,0},{32,8},{40,16},{48,24},{56,32},{64... | collective-permute-start | bytes 98312 | tf_op jit(solution)/shard_map/ppermute | solution.py:34
  27.1 51.0 %collective-permute-start.3 = (bf16[1024,16]{0,1:T(8,128)(2,1)}, bf16[1024,16]{0,1:T(8,128)(2,1)S(1)}, u32[]{:S(2)}, u32[]{:S(2)}) collective-permute-start(bf16[1024,16]{0,1:T(8,128)(2,1)} %param.14), channel_id=1, source_target_pairs={{0,96},{8,104},{16,112},{24,120},{32,0},{40,8},{48,16},{56,24},{64... | collective-permute-start | bytes 98312 | tf_op jit(solution)/shard_map/ppermute | solution.py:34
  30.0 51.2 %collective-permute-start.4 = (bf16[1024,16]{0,1:T(8,128)(2,1)}, bf16[1024,16]{0,1:T(8,128)(2,1)S(1)}, u32[]{:S(2)}, u32[]{:S(2)}) collective-permute-start(bf16[1024,16]{0,1:T(8,128)(2,1)} %param.14), channel_id=1, source_target_pairs={{0,88},{8,96},{16,104},{24,112},{32,120},{40,0},{48,8},{56,16},{64... | collective-permute-start | bytes 98312 | tf_op jit(solution)/shard_map/ppermute | solution.py:34
  34.2 88.7 %copy-start.4 = (bf16[384,128]{1,0:T(8,128)(2,1)S(1)}, bf16[384,128]{1,0:T(8,128)(2,1)}, u32[]{:S(2)}) copy-start(bf16[384,128]{1,0:T(8,128)(2,1)} %param.13) | copy-start | bytes 294916
  38.1 106.8 %all-to-all-start = ((bf16[64,3,1152]{2,1,0:T(4,128)(2,1)}), bf16[64,3,1152]{2,1,0:T(4,128)(2,1)S(1)}, u32[]{:S(2)}, u32[]{:S(2)}) async-start(bf16[64,3,1152]{2,1,0:T(4,128)(2,1)} %pad_maximum_fusion.1), calls=%async_computation.1 | async-start | bytes 1179648 | tf_op jit(solution)/shard_map/all_to_all | solution.py:89
  54.0 37.5 %collective-permute-start.5 = (bf16[1024,16]{0,1:T(8,128)(2,1)S(1)}, bf16[1024,16]{0,1:T(8,128)(2,1)S(1)}, u32[]{:S(2)}, u32[]{:S(2)}) collective-permute-start(bf16[1024,16]{0,1:T(8,128)(2,1)S(1)} %copy-done.3), channel_id=1, source_target_pairs={{0,80},{8,88},{16,96},{24,104},{32,112},{40,120},{48,0},{56,8},{64... | collective-permute-start | bytes 98312 | tf_op jit(solution)/shard_map/ppermute | solution.py:34
  64.4 33.8 %collective-permute-start.6 = (bf16[1024,16]{0,1:T(8,128)(2,1)S(1)}, bf16[1024,16]{0,1:T(8,128)(2,1)S(1)}, u32[]{:S(2)}, u32[]{:S(2)}) collective-permute-start(bf16[1024,16]{0,1:T(8,128)(2,1)S(1)} %copy-done.3), channel_id=1, source_target_pairs={{0,72},{8,80},{16,88},{24,96},{32,104},{40,112},{48,120},{56,0},{6... | collective-permute-start | bytes 98312 | tf_op jit(solution)/shard_map/ppermute | solution.py:34
  68.7 31.5 %collective-permute-start.7 = (bf16[1024,16]{0,1:T(8,128)(2,1)S(1)}, bf16[1024,16]{0,1:T(8,128)(2,1)S(1)}, u32[]{:S(2)}, u32[]{:S(2)}) collective-permute-start(bf16[1024,16]{0,1:T(8,128)(2,1)S(1)} %copy-done.3), channel_id=1, source_target_pairs={{0,64},{8,72},{16,80},{24,88},{32,96},{40,104},{48,112},{56,120},{... | collective-permute-start | bytes 98312 | tf_op jit(solution)/shard_map/ppermute | solution.py:34
  78.1 27.3 %collective-permute-start.8 = (bf16[1024,16]{0,1:T(8,128)(2,1)S(1)}, bf16[1024,16]{0,1:T(8,128)(2,1)S(1)}, u32[]{:S(2)}, u32[]{:S(2)}) collective-permute-start(bf16[1024,16]{0,1:T(8,128)(2,1)S(1)} %copy-done.3), channel_id=1, source_target_pairs={{0,56},{8,64},{16,72},{24,80},{32,88},{40,96},{48,104},{56,112},{6... | collective-permute-start | bytes 98312 | tf_op jit(solution)/shard_map/ppermute | solution.py:34
  81.2 26.9 %collective-permute-start.9 = (bf16[1024,16]{0,1:T(8,128)(2,1)S(1)}, bf16[1024,16]{0,1:T(8,128)(2,1)S(1)}, u32[]{:S(2)}, u32[]{:S(2)}) collective-permute-start(bf16[1024,16]{0,1:T(8,128)(2,1)S(1)} %copy-done.3), channel_id=1, source_target_pairs={{0,48},{8,56},{16,64},{24,72},{32,80},{40,88},{48,96},{56,104},{64... | collective-permute-start | bytes 98312 | tf_op jit(solution)/shard_map/ppermute | solution.py:34
  91.5 21.4 %collective-permute-start.10 = (bf16[1024,16]{0,1:T(8,128)(2,1)S(1)}, bf16[1024,16]{0,1:T(8,128)(2,1)S(1)}, u32[]{:S(2)}, u32[]{:S(2)}) collective-permute-start(bf16[1024,16]{0,1:T(8,128)(2,1)S(1)} %copy-done.3), channel_id=1, source_target_pairs={{0,40},{8,48},{16,56},{24,64},{32,72},{40,80},{48,88},{56,96},{64,... | collective-permute-start | bytes 98312 | tf_op jit(solution)/shard_map/ppermute | solution.py:34
  98.2 14.7 %collective-permute-start.11 = (bf16[1024,16]{0,1:T(8,128)(2,1)S(1)}, bf16[1024,16]{0,1:T(8,128)(2,1)S(1)}, u32[]{:S(2)}, u32[]{:S(2)}) collective-permute-start(bf16[1024,16]{0,1:T(8,128)(2,1)S(1)} %copy-done.3), channel_id=1, source_target_pairs={{0,32},{8,40},{16,48},{24,56},{32,64},{40,72},{48,80},{56,88},{64,... | collective-permute-start | bytes 98312 | tf_op jit(solution)/shard_map/ppermute | solution.py:34
  100.2 12.8 %collective-permute-start.12 = (bf16[1024,16]{0,1:T(8,128)(2,1)S(1)}, bf16[1024,16]{0,1:T(8,128)(2,1)S(1)}, u32[]{:S(2)}, u32[]{:S(2)}) collective-permute-start(bf16[1024,16]{0,1:T(8,128)(2,1)S(1)} %copy-done.3), channel_id=1, source_target_pairs={{0,24},{8,32},{16,40},{24,48},{32,56},{40,64},{48,72},{56,80},{64,... | collective-permute-start | bytes 98312 | tf_op jit(solution)/shard_map/ppermute | solution.py:34
  105.5 7.9 %collective-permute-start.13 = (bf16[1024,16]{0,1:T(8,128)(2,1)S(1)}, bf16[1024,16]{0,1:T(8,128)(2,1)S(1)}, u32[]{:S(2)}, u32[]{:S(2)}) collective-permute-start(bf16[1024,16]{0,1:T(8,128)(2,1)S(1)} %copy-done.3), channel_id=1, source_target_pairs={{0,16},{8,24},{16,32},{24,40},{32,48},{40,56},{48,64},{56,72},{64,... | collective-permute-start | bytes 98312 | tf_op jit(solution)/shard_map/ppermute | solution.py:34
  108.1 7.0 %collective-permute-start.14 = (bf16[1024,16]{0,1:T(8,128)(2,1)S(1)}, bf16[1024,16]{0,1:T(8,128)(2,1)S(1)}, u32[]{:S(2)}, u32[]{:S(2)}) collective-permute-start(bf16[1024,16]{0,1:T(8,128)(2,1)S(1)} %copy-done.3), channel_id=1, source_target_pairs={{0,8},{8,16},{16,24},{24,32},{32,40},{40,48},{48,56},{56,64},{64,7... | collective-permute-start | bytes 98312 | tf_op jit(solution)/shard_map/ppermute | solution.py:34
  115.4 22.0 %collective-permute-start.15 = (bf16[1024,256]{0,1:T(8,128)(2,1)S(1)}, bf16[1024,256]{0,1:T(8,128)(2,1)S(1)}, u32[]{:S(2)}, u32[]{:S(2)}) collective-permute-start(bf16[1024,256]{0,1:T(8,128)(2,1)S(1)} %bitcast.143), channel_id=1, source_target_pairs={{0,384},{128,0},{256,128},{384,256},{1,385},{129,1},{257,129},{385... | collective-permute-start | bytes 1572872 | tf_op jit(solution)/shard_map/ppermute | solution.py:34
  120.3 17.2 %collective-permute-start.16 = (bf16[1024,256]{0,1:T(8,128)(2,1)S(1)}, bf16[1024,256]{0,1:T(8,128)(2,1)S(1)}, u32[]{:S(2)}, u32[]{:S(2)}) collective-permute-start(bf16[1024,256]{0,1:T(8,128)(2,1)S(1)} %bitcast.144), channel_id=1, source_target_pairs={{0,256},{128,384},{256,0},{384,128},{1,257},{129,385},{257,1},{385... | collective-permute-start | bytes 1572872 | tf_op jit(solution)/shard_map/ppermute | solution.py:34
  123.0 20.1 %collective-permute-start.17 = (bf16[1024,256]{0,1:T(8,128)(2,1)S(1)}, bf16[1024,256]{0,1:T(8,128)(2,1)S(1)}, u32[]{:S(2)}, u32[]{:S(2)}) collective-permute-start(bf16[1024,256]{0,1:T(8,128)(2,1)S(1)} %bitcast.145), channel_id=1, source_target_pairs={{0,128},{128,256},{256,384},{384,0},{1,129},{129,257},{257,385},{3... | collective-permute-start | bytes 1572872 | tf_op jit(solution)/shard_map/ppermute | solution.py:34
  176.1 70.4 %all-to-all-start.1 = ((f32[3,64,1152]{2,0,1:T(4,128)}), f32[3,64,1152]{2,0,1:T(4,128)S(1)}, u32[]{:S(2)}, u32[]{:S(2)}) async-start(f32[3,64,1152]{2,0,1:T(4,128)} %copy.83), calls=%async_computation.2 | async-start | bytes 2359296 | tf_op jit(solution)/shard_map/all_to_all | solution.py:134
  186.3 43.7 %reduce-scatter.2.cloned.1.call-start = ((), (), s32[]{:S(2)}) async-start(), calls=%async_computation.3 | async-start | bytes 1769472 | tf_op jit(solution)/shard_map/reduce_scatter | solution.py:101
  210.2 41.1 %copy-start.2 = (bf16[128,1,16,64]{0,3,2,1:T(8,128)(2,1)S(1)}, bf16[128,1,16,64]{0,3,2,1:T(8,128)(2,1)}, u32[]{:S(2)}) copy-start(bf16[128,1,16,64]{0,3,2,1:T(8,128)(2,1)} %param.15) | copy-start | bytes 786436
  246.5 7.4 %copy-start.1 = (bf16[128,1,128]{2,0,1:T(8,128)(2,1)S(1)}, bf16[128,1,128]{2,0,1:T(8,128)(2,1)}, u32[]{:S(2)}) copy-start(bf16[128,1,128]{2,0,1:T(8,128)(2,1)} %param.18) | copy-start | bytes 98308
  246.5 7.4 %copy-start.5 = (f32[128,1,128]{2,1,0:T(1,128)S(1)}, f32[128,1,128]{2,1,0:T(1,128)}, u32[]{:S(2)}) copy-start(f32[128,1,128]{2,1,0:T(1,128)} %param.19) | copy-start | bytes 196612
  246.5 7.4 %copy-start.6 = (f32[128,1,128]{2,1,0:T(1,128)S(1)}, f32[128,1,128]{2,1,0:T(1,128)}, u32[]{:S(2)}) copy-start(f32[128,1,128]{2,1,0:T(1,128)} %param.20) | copy-start | bytes 196612
  248.6 5.4 %slice-start = ((f32[192,1,1152]{2,1,0:T(1,128)}), f32[192,1,128]{2,1,0:T(1,128)S(1)}, s32[]{:S(2)}) async-start(f32[192,1,1152]{2,1,0:T(1,128)} %all_to_all.21), calls=%async_computation.4 | async-start | bytes 196608 | tf_op jit(solution)/shard_map/slice | solution.py:136
Sparse Core Ops, SparseCore 0:
  190.5 39.4 reduce-scatter.1
where the time goes:
time: 263 us; the launch traced here: 262 us
  starting transfers between devices  120 us (46%)
  waiting for transfers between devices  54 us (21%)
  blocking collectives  38 us (14%)
  local copies, waits for them, and re-layouts  16.4 us (6%)
  between operations  14.8 us (6%)
  matrix products  12.2 us (5%)
  other arithmetic  6.9 us (3%)
    ppermute x18, starting transfers between devices, gather_along(): got.append(lax.ppermute(piece, axis, pairs))  93.5 us
    psum x1, blocking collectives, shards(): down_sum = lax.psum(down_part, 'mp')  22.7 us
    reduce_scatter x1, waiting for transfers between devices, shards(): lax.psum_scatter(frozen_part, 'mp', scatter_dimension=1, tiled=True)  19.9 us
    ppermute x18, waiting for transfers between devices, gather_along(): got.append(lax.ppermute(piece, axis, pairs))  19.3 us
    all_to_all x1, starting transfers between devices, shards(): lax.all_to_all(sent, ADAPTER, split_axis=0, concat_axis=0, tiled=True)  15.8 us
    all_gather x1, blocking collectives, shards(): masked_full = lax.all_gather(masked_own, 'mp', axis=1, tiled=True)  15.3 us
    all_to_all x1, waiting for transfers between devices, shards(): lax.all_to_all(grads, ADAPTER, split_axis=1, concat_axis=0, tiled=True)  14.7 us
    all_to_all x1, starting transfers between devices, shards(): lax.all_to_all(grads, ADAPTER, split_axis=1, concat_axis=0, tiled=True)  10.2 us
  transfers between devices with their start and end apart: 21, of which 7 were waited for; matrix products, arithmetic and copies ran while one was open for 7% of the time, Pallas kernels for 0%

commit v1 on v0

--- a/solution.py
+++ b/solution.py
@@ -79,7 +79,15 @@
     my_lengths = lax.dynamic_slice_in_dim(tile_length, my_index * tiles_here, tiles_here)
     active_rows = (jnp.arange(TILE)[None, :] < my_lengths[:, None]).reshape(tok_count, 1)
     masked_own = cotangent * active_rows.astype(jnp.bfloat16)
-    masked_full = lax.all_gather(masked_own, "mp", axis=1, tiled=True)
+    masked_full = jnp.concatenate(
+        lax.all_to_all(
+            jnp.stack([masked_own for _ in range(lax.psum(1, axis_name="mp"))], 0),
+            "mp",
+            split_axis=0,
+            concat_axis=0,
+        ),
+        axis=1,
+    )
     n_adapter = tile_total // tiles_here
     row_part = down_store.shape[2]
     rank = down_store.shape[3]

time: 263 us -> 276 us (1.049)
  waiting for transfers between devices: 54 us -> 68.4 us
  blocking collectives: 38 us -> 25.3 us
  starting transfers between devices: 120 us -> 125 us
  local copies, waits for them, and re-layouts: 16.4 us -> 20.2 us
    reduce_scatter x1, waiting for transfers between devices: 19.9 us -> 35.5 us  [shards(): lax.psum_scatter(frozen_part, 'mp', scatter_dimension=1, tiled=True)]
    all_gather x1 -> x0, blocking collectives: 15.3 us -> none  [shards(): masked_full = lax.all_gather(masked_own, 'mp', axis=1, tiled=True)]
    all_to_all x0 -> x1, starting transfers between devices: none -> 4.78 us  [shards(): lax.all_to_all(jnp.stack([masked_own for _ in range(lax.psum(1, axis_name...]
  transfers between devices with their start and end apart: 21 -> 22, of which waited for: 7 -> 7; matrix products, arithmetic and copies ran while one was open for 7% -> 12% of each run, Pallas kernels for 0% -> 0%
where the time goes in v1:
time: 276 us; the launch traced here: 274 us
  starting transfers between devices  125 us (45%)
  waiting for transfers between devices  68.4 us (25%)
  blocking collectives  25.3 us (9%)
  local copies, waits for them, and re-layouts  20.2 us (7%)
  between operations  14.8 us (5%)
  matrix products  13.8 us (5%)
  other arithmetic  6.6 us (2%)
    ppermute x18, starting transfers between devices, gather_along(): got.append(lax.ppermute(piece, axis, pairs))  93.5 us
    reduce_scatter x1, waiting for transfers between devices, shards(): lax.psum_scatter(frozen_part, 'mp', scatter_dimension=1, tiled=True)  35.5 us
    psum x1, blocking collectives, shards(): down_sum = lax.psum(down_part, 'mp')  25.3 us
    ppermute x18, waiting for transfers between devices, gather_along(): got.append(lax.ppermute(piece, axis, pairs))  17.7 us
    all_to_all x1, starting transfers between devices, shards(): lax.all_to_all(sent, ADAPTER, split_axis=0, concat_axis=0, tiled=True)  15.8 us
    all_to_all x1, waiting for transfers between devices, shards(): lax.all_to_all(grads, ADAPTER, split_axis=1, concat_axis=0, tiled=True)  15.2 us
    all_to_all x1, starting transfers between devices, shards(): lax.all_to_all(grads, ADAPTER, split_axis=1, concat_axis=0, tiled=True)  10.6 us
  transfers between devices with their start and end apart: 22, of which 7 were waited for; matrix products, arithmetic and copies ran while one was open for 12% of the time, Pallas kernels for 0%

profile of v1, /device:TPU:6, one launch (start us, length us, event | category | flops | bytes accessed | tf_op | source)
XLA Modules:
  0.0 274.1 jit_solution(9231686534893310610)
XLA Ops:
  7.2 11.5 %collective-permute-start = (bf16[1024,16]{0,1:T(8,128)(2,1)}, bf16[1024,16]{0,1:T(8,128)(2,1)S(1)}, u32[]{:S(2)}, u32[]{:S(2)}) collective-permute-start(bf16[1024,16]{0,1:T(8,128)(2,1)} %param.14), channel_id=1, source_target_pairs={{0,120},{8,0},{16,8},{24,16},{32,24},{40,32},{48,40},{56,48},{64,5... | collective-permute-start | bytes 98312 | tf_op jit(solution)/shard_map/ppermute | solution.py:34
  18.7 3.4 %collective-permute-start.1 = (bf16[1024,16]{0,1:T(8,128)(2,1)}, bf16[1024,16]{0,1:T(8,128)(2,1)S(1)}, u32[]{:S(2)}, u32[]{:S(2)}) collective-permute-start(bf16[1024,16]{0,1:T(8,128)(2,1)} %param.14), channel_id=1, source_target_pairs={{0,112},{8,120},{16,0},{24,8},{32,16},{40,24},{48,32},{56,40},{64,... | collective-permute-start | bytes 98312 | tf_op jit(solution)/shard_map/ppermute | solution.py:34
  22.1 5.0 %collective-permute-start.2 = (bf16[1024,16]{0,1:T(8,128)(2,1)}, bf16[1024,16]{0,1:T(8,128)(2,1)S(1)}, u32[]{:S(2)}, u32[]{:S(2)}) collective-permute-start(bf16[1024,16]{0,1:T(8,128)(2,1)} %param.14), channel_id=1, source_target_pairs={{0,104},{8,112},{16,120},{24,0},{32,8},{40,16},{48,24},{56,32},{64... | collective-permute-start | bytes 98312 | tf_op jit(solution)/shard_map/ppermute | solution.py:34
  27.1 2.8 %collective-permute-start.3 = (bf16[1024,16]{0,1:T(8,128)(2,1)}, bf16[1024,16]{0,1:T(8,128)(2,1)S(1)}, u32[]{:S(2)}, u32[]{:S(2)}) collective-permute-start(bf16[1024,16]{0,1:T(8,128)(2,1)} %param.14), channel_id=1, source_target_pairs={{0,96},{8,104},{16,112},{24,120},{32,0},{40,8},{48,16},{56,24},{64... | collective-permute-start | bytes 98312 | tf_op jit(solution)/shard_map/ppermute | solution.py:34
  30.0 1.9 collective-permute-start.4
  38.1 15.8 %all-to-all-start = ((bf16[64,3,1152]{2,1,0:T(4,128)(2,1)}), bf16[64,3,1152]{2,1,0:T(4,128)(2,1)S(1)}, u32[]{:S(2)}, u32[]{:S(2)}) async-start(bf16[64,3,1152]{2,1,0:T(4,128)(2,1)} %pad_maximum_fusion.1), calls=%async_computation.1 | async-start | bytes 1179648 | tf_op jit(solution)/shard_map/all_to_all | solution.py:97
  54.0 10.4 %collective-permute-start.5 = (bf16[1024,16]{0,1:T(8,128)(2,1)S(1)}, bf16[1024,16]{0,1:T(8,128)(2,1)S(1)}, u32[]{:S(2)}, u32[]{:S(2)}) collective-permute-start(bf16[1024,16]{0,1:T(8,128)(2,1)S(1)} %copy-done.7), channel_id=1, source_target_pairs={{0,80},{8,88},{16,96},{24,104},{32,112},{40,120},{48,0},{56,8},{64... | collective-permute-start | bytes 98312 | tf_op jit(solution)/shard_map/ppermute | solution.py:34
  64.4 4.3 %collective-permute-start.6 = (bf16[1024,16]{0,1:T(8,128)(2,1)S(1)}, bf16[1024,16]{0,1:T(8,128)(2,1)S(1)}, u32[]{:S(2)}, u32[]{:S(2)}) collective-permute-start(bf16[1024,16]{0,1:T(8,128)(2,1)S(1)} %copy-done.7), channel_id=1, source_target_pairs={{0,72},{8,80},{16,88},{24,96},{32,104},{40,112},{48,120},{56,0},{6... | collective-permute-start | bytes 98312 | tf_op jit(solution)/shard_map/ppermute | solution.py:34
  68.7 9.4 %collective-permute-start.7 = (bf16[1024,16]{0,1:T(8,128)(2,1)S(1)}, bf16[1024,16]{0,1:T(8,128)(2,1)S(1)}, u32[]{:S(2)}, u32[]{:S(2)}) collective-permute-start(bf16[1024,16]{0,1:T(8,128)(2,1)S(1)} %copy-done.7), channel_id=1, source_target_pairs={{0,64},{8,72},{16,80},{24,88},{32,96},{40,104},{48,112},{56,120},{... | collective-permute-start | bytes 98312 | tf_op jit(solution)/shard_map/ppermute | solution.py:34
  78.1 3.1 %collective-permute-start.8 = (bf16[1024,16]{0,1:T(8,128)(2,1)S(1)}, bf16[1024,16]{0,1:T(8,128)(2,1)S(1)}, u32[]{:S(2)}, u32[]{:S(2)}) collective-permute-start(bf16[1024,16]{0,1:T(8,128)(2,1)S(1)} %copy-done.7), channel_id=1, source_target_pairs={{0,56},{8,64},{16,72},{24,80},{32,88},{40,96},{48,104},{56,112},{6... | collective-permute-start | bytes 98312 | tf_op jit(solution)/shard_map/ppermute | solution.py:34
  81.2 10.3 %collective-permute-start.9 = (bf16[1024,16]{0,1:T(8,128)(2,1)S(1)}, bf16[1024,16]{0,1:T(8,128)(2,1)S(1)}, u32[]{:S(2)}, u32[]{:S(2)}) collective-permute-start(bf16[1024,16]{0,1:T(8,128)(2,1)S(1)} %copy-done.7), channel_id=1, source_target_pairs={{0,48},{8,56},{16,64},{24,72},{32,80},{40,88},{48,96},{56,104},{64... | collective-permute-start | bytes 98312 | tf_op jit(solution)/shard_map/ppermute | solution.py:34
  91.5 6.7 %collective-permute-start.10 = (bf16[1024,16]{0,1:T(8,128)(2,1)S(1)}, bf16[1024,16]{0,1:T(8,128)(2,1)S(1)}, u32[]{:S(2)}, u32[]{:S(2)}) collective-permute-start(bf16[1024,16]{0,1:T(8,128)(2,1)S(1)} %copy-done.7), channel_id=1, source_target_pairs={{0,40},{8,48},{16,56},{24,64},{32,72},{40,80},{48,88},{56,96},{64,... | collective-permute-start | bytes 98312 | tf_op jit(solution)/shard_map/ppermute | solution.py:34
  98.2 1.9 collective-permute-start.11
  100.2 5.2 %collective-permute-start.12 = (bf16[1024,16]{0,1:T(8,128)(2,1)S(1)}, bf16[1024,16]{0,1:T(8,128)(2,1)S(1)}, u32[]{:S(2)}, u32[]{:S(2)}) collective-permute-start(bf16[1024,16]{0,1:T(8,128)(2,1)S(1)} %copy-done.7), channel_id=1, source_target_pairs={{0,24},{8,32},{16,40},{24,48},{32,56},{40,64},{48,72},{56,80},{64,... | collective-permute-start | bytes 98312 | tf_op jit(solution)/shard_map/ppermute | solution.py:34
  105.4 2.7 collective-permute-start.13
  108.1 4.8 %collective-permute-start.14 = (bf16[1024,16]{0,1:T(8,128)(2,1)S(1)}, bf16[1024,16]{0,1:T(8,128)(2,1)S(1)}, u32[]{:S(2)}, u32[]{:S(2)}) collective-permute-start(bf16[1024,16]{0,1:T(8,128)(2,1)S(1)} %copy-done.7), channel_id=1, source_target_pairs={{0,8},{8,16},{16,24},{24,32},{32,40},{40,48},{48,56},{56,64},{64,7... | collective-permute-start | bytes 98312 | tf_op jit(solution)/shard_map/ppermute | solution.py:34
  115.4 4.8 %collective-permute-start.15 = (bf16[1024,256]{0,1:T(8,128)(2,1)S(1)}, bf16[1024,256]{0,1:T(8,128)(2,1)S(1)}, u32[]{:S(2)}, u32[]{:S(2)}) collective-permute-start(bf16[1024,256]{0,1:T(8,128)(2,1)S(1)} %bitcast.147), channel_id=1, source_target_pairs={{0,384},{128,0},{256,128},{384,256},{1,385},{129,1},{257,129},{385... | collective-permute-start | bytes 1572872 | tf_op jit(solution)/shard_map/ppermute | solution.py:34
  120.3 2.5 collective-permute-start.16
  124.6 2.9 %collective-permute-start.17 = (bf16[1024,256]{0,1:T(8,128)(2,1)S(1)}, bf16[1024,256]{0,1:T(8,128)(2,1)S(1)}, u32[]{:S(2)}, u32[]{:S(2)}) collective-permute-start(bf16[1024,256]{0,1:T(8,128)(2,1)S(1)} %bitcast.149), channel_id=1, source_target_pairs={{0,128},{128,256},{256,384},{384,0},{1,129},{129,257},{257,385},{3... | collective-permute-start | bytes 1572872 | tf_op jit(solution)/shard_map/ppermute | solution.py:34
  127.6 9.9 %collective-permute-done.15 = bf16[1024,256]{0,1:T(8,128)(2,1)S(1)} collective-permute-done((bf16[1024,256]{0,1:T(8,128)(2,1)S(1)}, bf16[1024,256]{0,1:T(8,128)(2,1)S(1)}, u32[]{:S(2)}, u32[]{:S(2)}) %collective-permute-start.15) | collective-permute-done | bytes 524320 | tf_op jit(solution)/shard_map/ppermute | solution.py:34
  137.6 5.5 %collective-permute-done.17 = bf16[1024,256]{0,1:T(8,128)(2,1)S(1)} collective-permute-done((bf16[1024,256]{0,1:T(8,128)(2,1)S(1)}, bf16[1024,256]{0,1:T(8,128)(2,1)S(1)}, u32[]{:S(2)}, u32[]{:S(2)}) %collective-permute-start.17) | collective-permute-done | bytes 524320 | tf_op jit(solution)/shard_map/ppermute | solution.py:34
  143.5 1.8 stack.89
  145.4 4.8 %all-to-all-start.1 = ((bf16[8,384,128]{1,2,0:T(8,128)(2,1)}), bf16[8,384,128]{1,2,0:T(8,128)(2,1)}, u32[]{:S(2)}, u32[]{:S(2)}) async-start(bf16[8,384,128]{1,2,0:T(8,128)(2,1)} %stack.89), calls=%async_computation.2 | async-start | bytes 1572864 | tf_op jit(solution)/shard_map/all_to_all | solution.py:83
  155.2 25.3 %all-reduce.2 = (bf16[3,128,64]{1,2,0:T(8,128)(2,1)S(1)}, bf16[3,128,64]{1,2,0:T(8,128)(2,1)S(1)}) all-reduce(f32[3,128,64]{1,2,0:T(8,128)S(1)} %convolution_bitcast_fusion.2, f32[3,128,64]{1,2,0:T(8,128)} %convolution_multiply_fusion.2), channel_id=1, replica_groups=mesh['ay'=4,'az'=16,'mp'=8] {'mp'}, use_global_device_ids=true, to_apply=%region_2.3 | all-reduce | flops 49152 | bytes 294912 | tf_op jit(solution)/shard_map/psum | solution.py:113
  181.8 2.8 %copy.86 = f32[3,1024,64]{2,1,0:T(8,128)} copy(f32[3,1024,64]{1,2,0:T(8,128)} %convolution_bitcast_fusion.1) | data formatting | bytes 1572864 | tf_op jit(solution)/shard_map/ntd,ntr->ndr/dot_general | solution.py:133
  184.6 2.7 reshape.161
  190.3 10.6 %all-to-all-start.2 = ((f32[3,64,1152]{2,0,1:T(4,128)}), f32[3,64,1152]{2,0,1:T(4,128)}, u32[]{:S(2)}, u32[]{:S(2)}) async-start(f32[3,64,1152]{2,0,1:T(4,128)} %copy.87), calls=%async_computation.3 | async-start | bytes 2359296 | tf_op jit(solution)/shard_map/all_to_all | solution.py:142
  201.1 2.5 convolution_bitcast_fusion
  205.5 3.0 %fusion = bf16[384,1024]{1,0:T(8,128)(2,1)} fusion(f32[3,128,1024]{2,1,0:T(8,128)S(1)} %fusion.19, bf16[384,1024]{0,1:T(8,128)(2,1)} %bitcast.39, bf16[1024,1024]{0,1:T(8,128)(2,1)S(1)} %bitcast.143), kind=kOutput, calls=%fused_computation.3 | convolution fusion | flops 806092800 | bytes 5242880 | tf_op jit(solution)/shard_map/dot_general | solution.py:126
  208.5 35.5 %reduce-scatter.2.cloned.1.call-done = f32[384,128]{0,1:T(8,128)} async-done(((f32[384,1024]{0,1:T(8,128)}), f32[384,128]{0,1:T(8,128)}) %reduce-scatter.2.cloned.1.call-update) | async-done | bytes 196624 | tf_op jit(solution)/shard_map/reduce_scatter | solution.py:109
  245.7 15.2 %all-to-all-done.2 = f32[3,64,1152]{2,0,1:T(4,128)} async-done(((f32[3,64,1152]{2,0,1:T(4,128)}), f32[3,64,1152]{2,0,1:T(4,128)}, u32[]{:S(2)}, u32[]{:S(2)}) %all-to-all-start.2) | async-done | bytes 884768 | tf_op jit(solution)/shard_map/all_to_all | solution.py:142
  260.9 2.3 all_to_all.25
  (117 shorter events, 28.0 us)
Async XLA Ops:
  7.2 146.5 %copy-start = (bf16[384,1024]{1,0:T(8,128)(2,1)S(1)}, bf16[384,1024]{1,0:T(8,128)(2,1)}, u32[]{:S(2)}) copy-start(bf16[384,1024]{1,0:T(8,128)(2,1)} %param.12) | copy-start | bytes 2359300
  7.2 46.6 %copy-start.7 = (bf16[1024,16]{0,1:T(8,128)(2,1)S(1)}, bf16[1024,16]{0,1:T(8,128)(2,1)}, u32[]{:S(2)}) copy-start(bf16[1024,16]{0,1:T(8,128)(2,1)} %param.14) | copy-start | bytes 98308
  7.2 46.7 %copy-start.10 = (s32[192]{0:T(256)S(1)}, s32[192]{0:T(256)}, u32[]{:S(2)}) copy-start(s32[192]{0:T(256)} %param.22) | copy-start | bytes 2308
  7.2 46.8 %collective-permute-start = (bf16[1024,16]{0,1:T(8,128)(2,1)}, bf16[1024,16]{0,1:T(8,128)(2,1)S(1)}, u32[]{:S(2)}, u32[]{:S(2)}) collective-permute-start(bf16[1024,16]{0,1:T(8,128)(2,1)} %param.14), channel_id=1, source_target_pairs={{0,120},{8,0},{16,8},{24,16},{32,24},{40,32},{48,40},{56,48},{64,5... | collective-permute-start | bytes 98312 | tf_op jit(solution)/shard_map/ppermute | solution.py:34
  18.7 45.6 %collective-permute-start.1 = (bf16[1024,16]{0,1:T(8,128)(2,1)}, bf16[1024,16]{0,1:T(8,128)(2,1)S(1)}, u32[]{:S(2)}, u32[]{:S(2)}) collective-permute-start(bf16[1024,16]{0,1:T(8,128)(2,1)} %param.14), channel_id=1, source_target_pairs={{0,112},{8,120},{16,0},{24,8},{32,16},{40,24},{48,32},{56,40},{64,... | collective-permute-start | bytes 98312 | tf_op jit(solution)/shard_map/ppermute | solution.py:34
  22.1 46.6 %collective-permute-start.2 = (bf16[1024,16]{0,1:T(8,128)(2,1)}, bf16[1024,16]{0,1:T(8,128)(2,1)S(1)}, u32[]{:S(2)}, u32[]{:S(2)}) collective-permute-start(bf16[1024,16]{0,1:T(8,128)(2,1)} %param.14), channel_id=1, source_target_pairs={{0,104},{8,112},{16,120},{24,0},{32,8},{40,16},{48,24},{56,32},{64... | collective-permute-start | bytes 98312 | tf_op jit(solution)/shard_map/ppermute | solution.py:34
  27.1 51.0 %collective-permute-start.3 = (bf16[1024,16]{0,1:T(8,128)(2,1)}, bf16[1024,16]{0,1:T(8,128)(2,1)S(1)}, u32[]{:S(2)}, u32[]{:S(2)}) collective-permute-start(bf16[1024,16]{0,1:T(8,128)(2,1)} %param.14), channel_id=1, source_target_pairs={{0,96},{8,104},{16,112},{24,120},{32,0},{40,8},{48,16},{56,24},{64... | collective-permute-start | bytes 98312 | tf_op jit(solution)/shard_map/ppermute | solution.py:34
  30.0 51.2 %collective-permute-start.4 = (bf16[1024,16]{0,1:T(8,128)(2,1)}, bf16[1024,16]{0,1:T(8,128)(2,1)S(1)}, u32[]{:S(2)}, u32[]{:S(2)}) collective-permute-start(bf16[1024,16]{0,1:T(8,128)(2,1)} %param.14), channel_id=1, source_target_pairs={{0,88},{8,96},{16,104},{24,112},{32,120},{40,0},{48,8},{56,16},{64... | collective-permute-start | bytes 98312 | tf_op jit(solution)/shard_map/ppermute | solution.py:34
  38.1 105.5 %all-to-all-start = ((bf16[64,3,1152]{2,1,0:T(4,128)(2,1)}), bf16[64,3,1152]{2,1,0:T(4,128)(2,1)S(1)}, u32[]{:S(2)}, u32[]{:S(2)}) async-start(bf16[64,3,1152]{2,1,0:T(4,128)(2,1)} %pad_maximum_fusion.1), calls=%async_computation.1 | async-start | bytes 1179648 | tf_op jit(solution)/shard_map/all_to_all | solution.py:97
  54.0 37.5 %collective-permute-start.5 = (bf16[1024,16]{0,1:T(8,128)(2,1)S(1)}, bf16[1024,16]{0,1:T(8,128)(2,1)S(1)}, u32[]{:S(2)}, u32[]{:S(2)}) collective-permute-start(bf16[1024,16]{0,1:T(8,128)(2,1)S(1)} %copy-done.7), channel_id=1, source_target_pairs={{0,80},{8,88},{16,96},{24,104},{32,112},{40,120},{48,0},{56,8},{64... | collective-permute-start | bytes 98312 | tf_op jit(solution)/shard_map/ppermute | solution.py:34
  64.4 33.8 %collective-permute-start.6 = (bf16[1024,16]{0,1:T(8,128)(2,1)S(1)}, bf16[1024,16]{0,1:T(8,128)(2,1)S(1)}, u32[]{:S(2)}, u32[]{:S(2)}) collective-permute-start(bf16[1024,16]{0,1:T(8,128)(2,1)S(1)} %copy-done.7), channel_id=1, source_target_pairs={{0,72},{8,80},{16,88},{24,96},{32,104},{40,112},{48,120},{56,0},{6... | collective-permute-start | bytes 98312 | tf_op jit(solution)/shard_map/ppermute | solution.py:34
  68.7 31.5 %collective-permute-start.7 = (bf16[1024,16]{0,1:T(8,128)(2,1)S(1)}, bf16[1024,16]{0,1:T(8,128)(2,1)S(1)}, u32[]{:S(2)}, u32[]{:S(2)}) collective-permute-start(bf16[1024,16]{0,1:T(8,128)(2,1)S(1)} %copy-done.7), channel_id=1, source_target_pairs={{0,64},{8,72},{16,80},{24,88},{32,96},{40,104},{48,112},{56,120},{... | collective-permute-start | bytes 98312 | tf_op jit(solution)/shard_map/ppermute | solution.py:34
  78.1 27.3 %collective-permute-start.8 = (bf16[1024,16]{0,1:T(8,128)(2,1)S(1)}, bf16[1024,16]{0,1:T(8,128)(2,1)S(1)}, u32[]{:S(2)}, u32[]{:S(2)}) collective-permute-start(bf16[1024,16]{0,1:T(8,128)(2,1)S(1)} %copy-done.7), channel_id=1, source_target_pairs={{0,56},{8,64},{16,72},{24,80},{32,88},{40,96},{48,104},{56,112},{6... | collective-permute-start | bytes 98312 | tf_op jit(solution)/shard_map/ppermute | solution.py:34
  81.2 26.9 %collective-permute-start.9 = (bf16[1024,16]{0,1:T(8,128)(2,1)S(1)}, bf16[1024,16]{0,1:T(8,128)(2,1)S(1)}, u32[]{:S(2)}, u32[]{:S(2)}) collective-permute-start(bf16[1024,16]{0,1:T(8,128)(2,1)S(1)} %copy-done.7), channel_id=1, source_target_pairs={{0,48},{8,56},{16,64},{24,72},{32,80},{40,88},{48,96},{56,104},{64... | collective-permute-start | bytes 98312 | tf_op jit(solution)/shard_map/ppermute | solution.py:34
  91.5 21.4 %collective-permute-start.10 = (bf16[1024,16]{0,1:T(8,128)(2,1)S(1)}, bf16[1024,16]{0,1:T(8,128)(2,1)S(1)}, u32[]{:S(2)}, u32[]{:S(2)}) collective-permute-start(bf16[1024,16]{0,1:T(8,128)(2,1)S(1)} %copy-done.7), channel_id=1, source_target_pairs={{0,40},{8,48},{16,56},{24,64},{32,72},{40,80},{48,88},{56,96},{64,... | collective-permute-start | bytes 98312 | tf_op jit(solution)/shard_map/ppermute | solution.py:34
  98.2 14.7 %collective-permute-start.11 = (bf16[1024,16]{0,1:T(8,128)(2,1)S(1)}, bf16[1024,16]{0,1:T(8,128)(2,1)S(1)}, u32[]{:S(2)}, u32[]{:S(2)}) collective-permute-start(bf16[1024,16]{0,1:T(8,128)(2,1)S(1)} %copy-done.7), channel_id=1, source_target_pairs={{0,32},{8,40},{16,48},{24,56},{32,64},{40,72},{48,80},{56,88},{64,... | collective-permute-start | bytes 98312 | tf_op jit(solution)/shard_map/ppermute | solution.py:34
  100.2 12.8 %collective-permute-start.12 = (bf16[1024,16]{0,1:T(8,128)(2,1)S(1)}, bf16[1024,16]{0,1:T(8,128)(2,1)S(1)}, u32[]{:S(2)}, u32[]{:S(2)}) collective-permute-start(bf16[1024,16]{0,1:T(8,128)(2,1)S(1)} %copy-done.7), channel_id=1, source_target_pairs={{0,24},{8,32},{16,40},{24,48},{32,56},{40,64},{48,72},{56,80},{64,... | collective-permute-start | bytes 98312 | tf_op jit(solution)/shard_map/ppermute | solution.py:34
  105.4 7.9 %collective-permute-start.13 = (bf16[1024,16]{0,1:T(8,128)(2,1)S(1)}, bf16[1024,16]{0,1:T(8,128)(2,1)S(1)}, u32[]{:S(2)}, u32[]{:S(2)}) collective-permute-start(bf16[1024,16]{0,1:T(8,128)(2,1)S(1)} %copy-done.7), channel_id=1, source_target_pairs={{0,16},{8,24},{16,32},{24,40},{32,48},{40,56},{48,64},{56,72},{64,... | collective-permute-start | bytes 98312 | tf_op jit(solution)/shard_map/ppermute | solution.py:34
  108.1 7.0 %collective-permute-start.14 = (bf16[1024,16]{0,1:T(8,128)(2,1)S(1)}, bf16[1024,16]{0,1:T(8,128)(2,1)S(1)}, u32[]{:S(2)}, u32[]{:S(2)}) collective-permute-start(bf16[1024,16]{0,1:T(8,128)(2,1)S(1)} %copy-done.7), channel_id=1, source_target_pairs={{0,8},{8,16},{16,24},{24,32},{32,40},{40,48},{48,56},{56,64},{64,7... | collective-permute-start | bytes 98312 | tf_op jit(solution)/shard_map/ppermute | solution.py:34
  115.4 22.0 %collective-permute-start.15 = (bf16[1024,256]{0,1:T(8,128)(2,1)S(1)}, bf16[1024,256]{0,1:T(8,128)(2,1)S(1)}, u32[]{:S(2)}, u32[]{:S(2)}) collective-permute-start(bf16[1024,256]{0,1:T(8,128)(2,1)S(1)} %bitcast.147), channel_id=1, source_target_pairs={{0,384},{128,0},{256,128},{384,256},{1,385},{129,1},{257,129},{385... | collective-permute-start | bytes 1572872 | tf_op jit(solution)/shard_map/ppermute | solution.py:34
  120.3 17.2 %collective-permute-start.16 = (bf16[1024,256]{0,1:T(8,128)(2,1)S(1)}, bf16[1024,256]{0,1:T(8,128)(2,1)S(1)}, u32[]{:S(2)}, u32[]{:S(2)}) collective-permute-start(bf16[1024,256]{0,1:T(8,128)(2,1)S(1)} %bitcast.148), channel_id=1, source_target_pairs={{0,256},{128,384},{256,0},{384,128},{1,257},{129,385},{257,1},{385... | collective-permute-start | bytes 1572872 | tf_op jit(solution)/shard_map/ppermute | solution.py:34
  124.6 18.5 %collective-permute-start.17 = (bf16[1024,256]{0,1:T(8,128)(2,1)S(1)}, bf16[1024,256]{0,1:T(8,128)(2,1)S(1)}, u32[]{:S(2)}, u32[]{:S(2)}) collective-permute-start(bf16[1024,256]{0,1:T(8,128)(2,1)S(1)} %bitcast.149), channel_id=1, source_target_pairs={{0,128},{128,256},{256,384},{384,0},{1,129},{129,257},{257,385},{3... | collective-permute-start | bytes 1572872 | tf_op jit(solution)/shard_map/ppermute | solution.py:34
  145.4 44.9 %all-to-all-start.1 = ((bf16[8,384,128]{1,2,0:T(8,128)(2,1)}), bf16[8,384,128]{1,2,0:T(8,128)(2,1)}, u32[]{:S(2)}, u32[]{:S(2)}) async-start(bf16[8,384,128]{1,2,0:T(8,128)(2,1)} %stack.89), calls=%async_computation.2 | async-start | bytes 1572864 | tf_op jit(solution)/shard_map/all_to_all | solution.py:83
  153.6 33.6 %copy-start.3 = (bf16[384,128]{1,0:T(8,128)(2,1)S(1)}, bf16[384,128]{1,0:T(8,128)(2,1)}, u32[]{:S(2)}) copy-start(bf16[384,128]{1,0:T(8,128)(2,1)} %copy-done.2) | copy-start | bytes 294916
  190.3 70.7 %all-to-all-start.2 = ((f32[3,64,1152]{2,0,1:T(4,128)}), f32[3,64,1152]{2,0,1:T(4,128)}, u32[]{:S(2)}, u32[]{:S(2)}) async-start(f32[3,64,1152]{2,0,1:T(4,128)} %copy.87), calls=%async_computation.3 | async-start | bytes 2359296 | tf_op jit(solution)/shard_map/all_to_all | solution.py:142
  200.9 43.2 %reduce-scatter.2.cloned.1.call-start = ((), (), s32[]{:S(2)}) async-start(), calls=%async_computation.4 | async-start | bytes 1769472 | tf_op jit(solution)/shard_map/reduce_scatter | solution.py:109
  208.5 56.4 %copy-start.4 = (bf16[128,1,16,64]{0,3,2,1:T(8,128)(2,1)S(1)}, bf16[128,1,16,64]{0,3,2,1:T(8,128)(2,1)}, u32[]{:S(2)}) copy-start(bf16[128,1,16,64]{0,3,2,1:T(8,128)(2,1)} %param.15) | copy-start | bytes 786436
  208.5 56.4 %copy-start.5 = (f32[128,1,16,64]{0,3,2,1:T(8,128)S(1)}, f32[128,1,16,64]{0,3,2,1:T(8,128)}, u32[]{:S(2)}) copy-start(f32[128,1,16,64]{0,3,2,1:T(8,128)} %param.16) | copy-start | bytes 1572868
  208.5 56.4 %copy-start.6 = (f32[128,1,16,64]{0,3,2,1:T(8,128)S(1)}, f32[128,1,16,64]{0,3,2,1:T(8,128)}, u32[]{:S(2)}) copy-start(f32[128,1,16,64]{0,3,2,1:T(8,128)} %param.17) | copy-start | bytes 1572868
  260.9 5.4 %copy-start.1 = (bf16[128,1,128]{2,0,1:T(8,128)(2,1)S(1)}, bf16[128,1,128]{2,0,1:T(8,128)(2,1)}, u32[]{:S(2)}) copy-start(bf16[128,1,128]{2,0,1:T(8,128)(2,1)} %param.18) | copy-start | bytes 98308
  260.9 5.4 %copy-start.8 = (f32[128,1,128]{2,1,0:T(1,128)S(1)}, f32[128,1,128]{2,1,0:T(1,128)}, u32[]{:S(2)}) copy-start(f32[128,1,128]{2,1,0:T(1,128)} %param.19) | copy-start | bytes 196612
  260.9 5.4 %copy-start.9 = (f32[128,1,128]{2,1,0:T(1,128)S(1)}, f32[128,1,128]{2,1,0:T(1,128)}, u32[]{:S(2)}) copy-start(f32[128,1,128]{2,1,0:T(1,128)} %param.20) | copy-start | bytes 196612
  (1 other events, 0.8 us)
Sparse Core Ops, SparseCore 0:
  204.5 39.4 reduce-scatter.1
